TPU v7x, 256 devices: a whole 4x4x8 slice. The times are simulated.
256 devices in a mesh: dp: 64 (over x, z, core), pipe: 4 (over y).
Axes of the slice: x: 4, y: 4, z: 8, core: 2. Of those that a mesh axis runs over, the one named last changes fastest.
Arguments:
- tokens: bfloat16 [8192, 2560], P('dp'), may hold values from -6 to 6
- norm_gains: bfloat16 [4, 2560], P('pipe', 'dp'), may hold values from 0.099609375 to 1.8984375
- up_weights: bfloat16 [4, 64, 128, 128], P('pipe', 'dp'), may hold values from -0.5 to 0.5
- down_weights: bfloat16 [4, 64, 128, 128], P('pipe', 'dp'), may hold values from -0.3125 to 0.3125
- coords: int32 [4, 4, 64], P('pipe'), may hold values from 0 to 79, as said below
- cotangent: bfloat16 [8192, 2560], P('dp'), may hold values from -6 to 6
Outputs:
- grad_up: float32 [4, 64, 128, 128], P('pipe', 'dp')
- grad_down: float32 [4, 64, 128, 128], P('pipe', 'dp')
- grad_gain: float32 [4, 2560], P('pipe', 'dp')
- grad_inputs: bfloat16 [4, 8192, 2560], P('pipe', 'dp')
Inputs may be any that keep to these rules, and one draw needn't show every extreme that they name: For every layer the 64 pairs (coords[l,0,b], coords[l,1,b]) are distinct, and so are the pairs (coords[l,2,b], coords[l,3,b]); rows 0 and 3 lie below 20, rows 1 and 2 below 80.
All inputs are finite; a program needn't handle non-finite values.
Results may differ from a plain program's by a relative error of at most 0.011.
Values may be sent and summed in bfloat16 or wider, within the bound.
No kernel may reach another device: no remote copies, remote signals or barrier semaphores. Data moves between devices by JAX's collectives and lax.ppermute only.
A program may use at most 128 MiB of HBM per device.

v0:
```python
import math
import jax
import jax.numpy as jnp
from jax import lax
from jax.sharding import PartitionSpec as P

FF = 10240
MICRO = 2
epsilon = 1e-05


def from_behind(value, axis, by):
    size = lax.axis_size(axis)
    pairs = [(i, i + by) for i in range(size) if 0 <= i + by < size]
    return lax.ppermute(value, axis, pairs)


def norm_parts(inputs, gain_row):
    widened = inputs.astype(jnp.float32)
    inverse = lax.rsqrt(jnp.mean(widened * widened, axis=-1, keepdims=True) + epsilon)
    unit_rows = widened * inverse
    normed = (unit_rows * gain_row.astype(jnp.float32)).astype(jnp.bfloat16)
    return (widened, inverse, unit_rows, normed)


def to_panels(values, panel_width):
    row_count = values.shape[0]
    return jnp.transpose(values.reshape(row_count, -1, panel_width), (1, 0, 2))


def from_panels(panels):
    return jnp.transpose(panels, (1, 0, 2)).reshape(
        panels.shape[1], panels.shape[0] * panels.shape[2]
    )


def panel_product(panels, blocks, pick_index, put_index, put_count, form):
    picked = jnp.take(panels, pick_index, axis=0)
    products = jnp.einsum(form, picked, blocks, preferred_element_type=jnp.float32)
    placing = (put_index[:, None] == jnp.arange(put_count, dtype=jnp.int32)[None, :]).astype(
        jnp.float32
    )
    return jnp.einsum("brc,bp->prc", products, placing, precision=lax.Precision.HIGH)


def up_product(inputs, gain_row, up_blocks, block_links, hidden_panels, panel_width):
    normed = norm_parts(inputs, gain_row)[3]
    return panel_product(
        to_panels(normed, panel_width),
        up_blocks,
        block_links[0],
        block_links[1],
        hidden_panels,
        "bri,bio->bro",
    )


def layer_forward(
    inputs, gain_row, up_blocks, down_blocks, block_links, hidden_panels, model_panels, panel_width
):
    widened, inverse, unit_rows, normed = norm_parts(inputs, gain_row)
    before = panel_product(
        to_panels(normed, panel_width),
        up_blocks,
        block_links[0],
        block_links[1],
        hidden_panels,
        "bri,bio->bro",
    )
    active = jax.nn.gelu(before).astype(jnp.bfloat16)
    added = from_panels(
        panel_product(
            active, down_blocks, block_links[2], block_links[3], model_panels, "bri,bio->bro"
        )
    )
    return ((widened + added).astype(jnp.bfloat16), before)


def layer_backward(
    inputs,
    upstream,
    before,
    gain_row,
    up_blocks,
    down_blocks,
    block_links,
    hidden_panels,
    model_panels,
    panel_width,
):
    widened, inverse, unit_rows, normed = norm_parts(inputs, gain_row)
    upstream_panels = to_panels(upstream, panel_width)
    active_full, gelu_slope = jax.jvp(jax.nn.gelu, (before,), (jnp.ones_like(before),))
    active = active_full.astype(jnp.bfloat16)
    grad_active = panel_product(
        upstream_panels, down_blocks, block_links[3], block_links[2], hidden_panels, "bro,bio->bri"
    )
    grad_before = (grad_active * gelu_slope).astype(jnp.bfloat16)
    grad_normed = from_panels(
        panel_product(
            grad_before, up_blocks, block_links[1], block_links[0], model_panels, "bro,bio->bri"
        )
    )
    gain_grad = jnp.sum(grad_normed * unit_rows, axis=0)
    grad_unit = grad_normed * gain_row.astype(jnp.float32)
    centered = grad_unit - unit_rows * jnp.mean(grad_unit * unit_rows, axis=-1, keepdims=True)
    grad_local = (upstream.astype(jnp.float32) + inverse * centered).astype(jnp.bfloat16)
    return (
        grad_local,
        gain_grad,
        to_panels(normed, panel_width),
        active,
        grad_before,
        upstream_panels,
    )


def own_slots(collected, first):
    stacked = jnp.stack(collected)
    return lax.dynamic_slice_in_dim(stacked, first, MICRO, 0)


def shards(tokens, norm_gains, up_weights, down_weights, coords, cotangent):
    phases = lax.axis_size("pipe")
    section = lax.axis_index("pipe")
    panel_width = up_weights.shape[2]
    model_width = tokens.shape[1]
    token_rows = tokens.shape[0]
    hidden_panels = FF // panel_width
    model_panels = model_width // panel_width
    group_rows = token_rows // MICRO
    block_links = coords[0]
    block_width = panel_width * panel_width
    gain_count = norm_gains.shape[1]
    gain_room = -(-gain_count // 128) * 128
    packed = jnp.concatenate(
        [
            up_weights.reshape(1, 1, block_width),
            down_weights.reshape(1, 1, block_width),
            jnp.pad(
                norm_gains.reshape(1, 1, gain_count), ((0, 0), (0, 0), (0, gain_room - gain_count))
            ),
        ],
        axis=2,
    )
    gathered = lax.all_gather(packed, "dp", axis=1, tiled=True)[0]
    block_count = gathered.shape[0]
    up_blocks = gathered[:, :block_width].reshape(block_count, panel_width, panel_width)
    down_blocks = gathered[:, block_width : 2 * block_width].reshape(
        block_count, panel_width, panel_width
    )
    gain_row = gathered[:, 2 * block_width : 2 * block_width + gain_count].reshape(-1)
    token_groups = tokens.reshape(MICRO, group_rows, model_width)
    cot_groups = cot_groups_of = cotangent.reshape(MICRO, group_rows, model_width)
    last_tick = MICRO + phases - 2
    input_list = []
    before_list = []
    arriving = jnp.zeros((group_rows, model_width), jnp.bfloat16)
    for moment in range(last_tick + 1):
        current = jnp.where(section == 0, token_groups[min(moment, MICRO - 1)], arriving)
        input_list.append(current)
        leaving, before = layer_forward(
            current,
            gain_row,
            up_blocks,
            down_blocks,
            block_links,
            hidden_panels,
            model_panels,
            panel_width,
        )
        before_list.append(before)
        if moment < last_tick:
            arriving = from_behind(leaving, "pipe", 1)
    input_stack = jnp.stack(input_list)
    before_stack = jnp.stack(before_list)
    gain_total = jnp.zeros((model_width,), jnp.float32)
    grad_list = []
    normed_list = []
    upper_list = []
    active_list = []
    slope_list = []
    arriving = jnp.zeros((group_rows, model_width), jnp.bfloat16)
    for moment in range(last_tick + 1):
        slot_index = moment - (phases - 1 - section)
        slot_live = (slot_index >= 0) & (slot_index < MICRO)
        tick_place = jnp.clip(slot_index, 0, MICRO - 1) + section
        upstream = jnp.where(section == phases - 1, cot_groups_of[min(moment, MICRO - 1)], arriving)
        inputs = lax.dynamic_index_in_dim(input_stack, tick_place, 0, keepdims=False)
        before = lax.dynamic_index_in_dim(before_stack, tick_place, 0, keepdims=False)
        grad_local, gain_grad, normed, active, grad_before, upper = layer_backward(
            inputs,
            upstream,
            before,
            gain_row,
            up_blocks,
            down_blocks,
            block_links,
            hidden_panels,
            model_panels,
            panel_width,
        )
        gain_total = gain_total + jnp.where(slot_live, gain_grad, 0.0)
        grad_list.append(grad_local)
        normed_list.append(normed)
        upper_list.append(upper)
        active_list.append(active)
        slope_list.append(grad_before)
        if moment < last_tick:
            arriving = from_behind(grad_local, "pipe", -1)
    first = phases - 1 - section
    grad_store = own_slots(grad_list, first)
    normed_all = own_slots(normed_list, first)
    upper_all = own_slots(upper_list, first)
    active_all = own_slots(active_list, first)
    slope_all = own_slots(slope_list, first)
    grad_scale = 1.0 / math.sqrt(token_rows * lax.axis_size("dp"))
    up_total = jnp.einsum(
        "mbri,mbro->bio",
        jnp.take(normed_all, block_links[0], axis=1),
        jnp.take(slope_all, block_links[1], axis=1),
        preferred_element_type=jnp.float32,
    )
    down_total = jnp.einsum(
        "mbri,mbro->bio",
        jnp.take(active_all, block_links[2], axis=1),
        jnp.take(upper_all, block_links[3], axis=1),
        preferred_element_type=jnp.float32,
    )
    gain_parts = jnp.pad(
        gain_total.reshape(block_count, gain_count), ((0, 0), (0, 8 * 128 - gain_count))
    )
    totals = jnp.concatenate(
        [
            up_total.reshape(block_count, block_width),
            down_total.reshape(block_count, block_width),
            gain_parts,
        ],
        axis=1,
    )
    summed = (
        lax.psum_scatter(
            totals.reshape(1, block_count, -1, 128), "dp", scatter_dimension=1, tiled=True
        ).reshape(-1)
        * grad_scale
    )
    up_out = summed[:block_width].reshape(1, 1, panel_width, panel_width)
    down_out = summed[block_width : 2 * block_width].reshape(1, 1, panel_width, panel_width)
    gain_out = summed[2 * block_width : 2 * block_width + gain_count].reshape(1, gain_count)
    return (up_out, down_out, gain_out, grad_store.reshape(1, token_rows, model_width))


def solution(mesh):
    in_specs = (
        P("dp", None),
        P("pipe", "dp"),
        P("pipe", "dp", None, None),
        P("pipe", "dp", None, None),
        P("pipe", None, None),
        P("dp", None),
    )
    out_specs = (
        P("pipe", "dp", None, None),
        P("pipe", "dp", None, None),
        P("pipe", "dp"),
        P("pipe", "dp", None),
    )
    return jax.shard_map(shards, mesh=mesh, in_specs=in_specs, out_specs=out_specs, check_vma=False)
```

profile of v0, /device:TPU:8, one launch (start us, length us, event | category | flops | bytes accessed | tf_op | source)
XLA Modules:
  0.0 626.4 jit_solution(7334065427860682173)
XLA Ops:
  12.9 84.3 %all-gather.2.cloned.1.call-done = bf16[1,64,32896]{2,0,1:T(2,128)(2,1)} async-done(((bf16[1,1,32896]{2,0,1:T(2,128)(2,1)}), bf16[1,64,32896]{2,0,1:T(2,128)(2,1)}) %all-gather.2.cloned.1.call-update) | async-done | bytes 4210704 | tf_op jit(solution)/shard_map/all_gather | solution.py:146
  97.2 3.8 copy.258
  109.6 3.5 bitcast_dynamic-update-slice_fusion.4
  117.2 3.0 gather_fusion.1
  124.6 3.6 collective-permute-start
  129.0 7.3 %collective-permute-done = bf16[64,2560]{1,0:T(8,128)(2,1)S(1)} collective-permute-done((bf16[64,2560]{1,0:T(8,128)(2,1)S(1)}, bf16[64,2560]{1,0:T(8,128)(2,1)S(1)}, u32[]{:S(2)}, u32[]{:S(2)}) %collective-permute-start) | collective-permute-done | bytes 327712 | tf_op jit(solution)/shard_map/ppermute | solution.py:15
  141.2 3.5 bitcast_dynamic-update-slice_fusion.3
  147.0 3.0 gather_fusion.3
  155.1 3.6 collective-permute-start.1
  159.6 6.8 %collective-permute-done.1 = bf16[64,2560]{1,0:T(8,128)(2,1)} collective-permute-done((bf16[64,2560]{1,0:T(8,128)(2,1)}, bf16[64,2560]{1,0:T(8,128)(2,1)}, u32[]{:S(2)}, u32[]{:S(2)}) %collective-permute-start.1) | collective-permute-done | bytes 327712 | tf_op jit(solution)/shard_map/ppermute | solution.py:15
  174.4 3.5 bitcast_dynamic-update-slice_fusion.2
  180.2 3.0 gather_fusion.5
  188.3 3.6 collective-permute-start.2
  206.6 3.6 bitcast_dynamic-update-slice_fusion.1
  212.4 3.0 gather_fusion.7
  219.8 3.9 collective-permute-start.3
  223.7 2.9 fusion.222
  233.7 3.6 bitcast_dynamic-update-slice_fusion
  237.3 3.8 fusion.201
  241.2 6.7 %bitcast_dynamic-update-slice_fusion.9 = (bf16[5,80,64,128]{3,1,2,0:T(8,128)(2,1)}, bf16[80,64,128]{2,0,1:T(8,128)(2,1)S(1)}) fusion(f32[5,80,64,128]{3,1,2,0:T(8,128)} %bitcast_dynamic-update-slice_fusion, s32[]{:T(128)S(6)} %select_n.163, f32[64,64,128]{2,1,0:T(8,128)S(1)} %copy-done.25, s32[64]{0:T(128)S(1)} %get-tuple-element.59), kind=kOutput, calls=%fused_computation.248 | convolution fusion | flops 263459840 | bytes 7340292 | tf_op jit(solution)/shard_map/brc,bp->prc/dot_general | solution.py:43
  255.2 3.1 gather_fusion.11
  271.1 3.2 dynamic-slice_convert_fusion
  281.1 3.7 fusion.200
  284.8 3.7 fusion.199
  288.5 3.8 fusion.198
  294.1 3.7 fusion.197
  305.1 3.5 fusion.216
  308.6 6.9 %bitcast_dynamic-update-slice_fusion.8 = (bf16[5,80,64,128]{3,1,2,0:T(8,128)(2,1)}, bf16[80,64,128]{2,0,1:T(8,128)(2,1)S(1)}) fusion(bf16[5,80,64,128]{3,1,2,0:T(8,128)(2,1)} %get-tuple-element.79, f32[5,80,64,128]{3,1,2,0:T(8,128)} %bitcast_dynamic-update-slice_fusion, s32[]{:T(128)S(6)} %select_n.164, f32[64,64,128]{2,1,0:T(8,128)S(1)} %fusion.216, ...), kind=kOutput, calls=%fused_computation.247 | convolution fusion | flops 263459840 | bytes 7340292 | tf_op jit(solution)/shard_map/brc,bp->prc/dot_general | solution.py:43
  316.9 3.1 gather_fusion.13
  329.9 3.4 constant_dynamic-slice_fusion.2
  342.0 3.5 fusion.212
  345.5 6.9 %bitcast_dynamic-update-slice_fusion.7 = (bf16[5,80,64,128]{3,1,2,0:T(8,128)(2,1)}, bf16[80,64,128]{2,0,1:T(8,128)(2,1)S(1)}) fusion(bf16[5,80,64,128]{3,1,2,0:T(8,128)(2,1)} %get-tuple-element.81, f32[5,80,64,128]{3,1,2,0:T(8,128)} %bitcast_dynamic-update-slice_fusion, s32[]{:T(128)S(6)} %select_n.165, f32[64,64,128]{2,1,0:T(8,128)S(1)} %fusion.212, ...), kind=kOutput, calls=%fused_computation.246 | convolution fusion | flops 263459840 | bytes 7340292 | tf_op jit(solution)/shard_map/brc,bp->prc/dot_general | solution.py:43
  353.8 3.0 gather_fusion.15
  369.8 3.9 copy.116
  373.7 4.0 gather_fusion.20
  382.4 3.5 fusion.208
  385.8 7.1 %bitcast_dynamic-update-slice_fusion.6 = (bf16[5,80,64,128]{3,1,2,0:T(8,128)(2,1)}, bf16[80,64,128]{2,0,1:T(8,128)(2,1)S(1)}) fusion(bf16[5,80,64,128]{3,1,2,0:T(8,128)(2,1)} %get-tuple-element.83, f32[5,80,64,128]{3,1,2,0:T(8,128)} %bitcast_dynamic-update-slice_fusion, s32[]{:T(128)S(6)} %select_n.166, f32[64,64,128]{2,1,0:T(8,128)S(1)} %fusion.208, ...), kind=kOutput, calls=%fused_computation.245 | convolution fusion | flops 263459840 | bytes 7340292 | tf_op jit(solution)/shard_map/brc,bp->prc/dot_general | solution.py:43
  394.4 3.0 gather_fusion.17
  410.2 3.4 collective-permute-done.7
  416.2 3.5 fusion.204
  419.7 6.8 %bitcast_dynamic-update-slice_fusion.5 = (bf16[5,80,64,128]{3,1,2,0:T(8,128)(2,1)}, bf16[80,64,128]{2,0,1:T(8,128)(2,1)S(1)}) fusion(bf16[5,80,64,128]{3,1,2,0:T(8,128)(2,1)} %get-tuple-element.85, f32[5,80,64,128]{3,1,2,0:T(8,128)} %bitcast_dynamic-update-slice_fusion, s32[]{:T(128)S(6)} %select_n.167, f32[64,64,128]{2,1,0:T(8,128)S(1)} %fusion.204, ...), kind=kOutput, calls=%fused_computation.244 | convolution fusion | flops 263459840 | bytes 7340292 | tf_op jit(solution)/shard_map/brc,bp->prc/dot_general | solution.py:43
  427.9 3.0 gather_fusion.22
  441.1 3.2 fusion.136
  444.4 4.4 copy.260
  454.0 4.6 copy.259
  458.8 3.8 fusion
  462.5 4.9 copy.145
  471.4 145.8 %reduce-scatter.5.cloned.1.call-done = f32[1,1,264,128]{3,2,1,0:T(8,128)} async-done(((f32[1,64,264,128]{3,2,1,0:T(8,128)}), f32[1,1,264,128]{3,2,1,0:T(8,128)}) %reduce-scatter.5.cloned.1.call-update) | async-done | bytes 135184
  (277 shorter events, 195.0 us)
Async XLA Ops:
  7.2 4.9 copy-start.2
  7.2 4.3 copy-start.48
  7.2 90.0 %all-gather.2.cloned.1.call-start = ((), (), s32[]{:S(2)}) async-start(), calls=%async_computation.1 | async-start | bytes 8552960 | tf_op jit(solution)/shard_map/all_gather | solution.py:146
  10.3 606.9 %reduce-scatter.5.cloned.1.call-start = ((), (), s32[]{:S(2)}) async-start(), calls=%async_computation.2 | async-start | bytes 8785920
  12.0 203.4 %copy-start.42 = (pred[64]{0:T(512)(128)(4,1)}, pred[64]{0:T(512)(128)(4,1)S(1)}, u32[]{:S(2)}) copy-start(pred[64]{0:T(512)(128)(4,1)S(1)} %get-tuple-element.60) | copy-start | bytes 196
  12.0 219.7 %copy-start.37 = (pred[64]{0:T(512)(128)(4,1)}, pred[64]{0:T(512)(128)(4,1)S(1)}, u32[]{:S(2)}) copy-start(pred[64]{0:T(512)(128)(4,1)S(1)} %get-tuple-element.62) | copy-start | bytes 196
  12.1 200.4 %copy-start.47 = (s32[1024]{0:T(1024)}, s32[1024]{0:T(1024)S(1)}, u32[]{:S(2)}) copy-start(s32[1024]{0:T(1024)S(1)} %get-tuple-element.91) | copy-start | bytes 12292
  12.1 218.0 %copy-start.44 = (s32[1024]{0:T(1024)}, s32[1024]{0:T(1024)S(1)}, u32[]{:S(2)}) copy-start(s32[1024]{0:T(1024)S(1)} %get-tuple-element.92) | copy-start | bytes 12292
  12.9 228.3 %copy-start.58 = (s32[64]{0:T(128)}, s32[64]{0:T(128)S(1)}, u32[]{:S(2)}) copy-start(s32[64]{0:T(128)S(1)} %get-tuple-element.59) | copy-start | bytes 772
  124.6 11.8 %collective-permute-start = (bf16[64,2560]{1,0:T(8,128)(2,1)S(1)}, bf16[64,2560]{1,0:T(8,128)(2,1)S(1)}, u32[]{:S(2)}, u32[]{:S(2)}) collective-permute-start(bf16[64,2560]{1,0:T(8,128)(2,1)S(1)} %fusion.309), channel_id=1, source_target_pairs={{0,1},{1,2},{2,3},{4,5},{5,6},{6,7},{8,9},{9,10},{10,11},{12,13},{... | collective-permute-start | bytes 983048 | tf_op jit(solution)/shard_map/ppermute | solution.py:15
  129.0 100.9 %copy-start.26 = (f32[2560]{0:T(1024)}, f32[2560]{0:T(1024)S(1)}, u32[]{:S(2)}) copy-start(f32[2560]{0:T(1024)S(1)} %reshape.565) | copy-start | bytes 30724
  137.2 4.0 copy-start.16
  152.6 6.1 copy-start.1
  155.1 11.3 %collective-permute-start.1 = (bf16[64,2560]{1,0:T(8,128)(2,1)}, bf16[64,2560]{1,0:T(8,128)(2,1)}, u32[]{:S(2)}, u32[]{:S(2)}) collective-permute-start(bf16[64,2560]{1,0:T(8,128)(2,1)} %fusion.282), channel_id=1, source_target_pairs={{0,1},{1,2},{2,3},{4,5},{5,6},{6,7},{8,9},{9,10},{10,11},{12,13},{... | collective-permute-start | bytes 983048 | tf_op jit(solution)/shard_map/ppermute | solution.py:15
  188.3 10.3 %collective-permute-start.2 = (bf16[64,2560]{1,0:T(8,128)(2,1)}, bf16[64,2560]{1,0:T(8,128)(2,1)}, u32[]{:S(2)}, u32[]{:S(2)}) collective-permute-start(bf16[64,2560]{1,0:T(8,128)(2,1)} %fusion.286), channel_id=1, source_target_pairs={{0,1},{1,2},{2,3},{4,5},{5,6},{6,7},{8,9},{9,10},{10,11},{12,13},{... | collective-permute-start | bytes 983048 | tf_op jit(solution)/shard_map/ppermute | solution.py:15
  192.5 12.1 %copy-start.45 = (s32[1024]{0:T(1024)}, s32[1024]{0:T(1024)S(1)}, u32[]{:S(2)}) copy-start(s32[1024]{0:T(1024)S(1)} %get-tuple-element.90) | copy-start | bytes 12292
  218.1 5.6 copy-start
  218.1 5.6 copy-start.20
  219.8 9.1 %collective-permute-start.3 = (bf16[64,2560]{1,0:T(8,128)(2,1)S(1)}, bf16[64,2560]{1,0:T(8,128)(2,1)S(1)}, u32[]{:S(2)}, u32[]{:S(2)}) collective-permute-start(bf16[64,2560]{1,0:T(8,128)(2,1)S(1)} %fusion.290), channel_id=1, source_target_pairs={{0,1},{1,2},{2,3},{4,5},{5,6},{6,7},{8,9},{9,10},{10,11},{12,13},{... | collective-permute-start | bytes 983048 | tf_op jit(solution)/shard_map/ppermute | solution.py:15
  237.3 3.8 copy-start.25
  258.3 3.7 copy-start.39
  261.1 4.6 copy-start.27
  264.9 6.2 copy-start.28
  264.9 6.2 copy-start.50
  267.7 32.8 %collective-permute-start.4 = (bf16[64,2560]{1,0:T(8,128)(2,1)}, bf16[64,2560]{1,0:T(8,128)(2,1)}, u32[]{:S(2)}, u32[]{:S(2)}) collective-permute-start(bf16[64,2560]{1,0:T(8,128)(2,1)} %fusion.276), channel_id=1, source_target_pairs={{1,0},{2,1},{3,2},{5,4},{6,5},{7,6},{9,8},{10,9},{11,10},{13,12},{... | collective-permute-start | bytes 983048 | tf_op jit(solution)/shard_map/ppermute | solution.py:15
  271.1 5.3 copy-start.57
  278.1 15.1 %copy-start.9 = (f32[64,20,128]{2,1,0:T(8,128)}, f32[64,20,128]{2,1,0:T(8,128)S(1)}, u32[]{:S(2)}) copy-start(f32[64,20,128]{2,1,0:T(8,128)S(1)} %reshape.570) | copy-start | bytes 1966084
  278.7 14.5 %copy-start.53 = (f32[64]{0:T(128)}, f32[64]{0:T(128)S(1)}, u32[]{:S(2)}) copy-start(f32[64]{0:T(128)S(1)} %add_rsqrt_fusion.3) | copy-start | bytes 772
  288.5 3.8 copy-start.11
  288.5 3.8 copy-start.55
  299.0 9.6 %copy-start.7 = (f32[64,20,128]{2,1,0:T(8,128)}, f32[64,20,128]{2,1,0:T(8,128)S(1)}, u32[]{:S(2)}) copy-start(f32[64,20,128]{2,1,0:T(8,128)S(1)} %reshape.572) | copy-start | bytes 1966084
  305.1 3.5 copy-start.59
  315.5 4.5 copy-start.35
  320.0 2.9 copy-start.40
  320.0 2.9 copy-start.56
  328.0 9.5 %collective-permute-start.5 = (bf16[64,2560]{1,0:T(8,128)(2,1)}, bf16[64,2560]{1,0:T(8,128)(2,1)}, u32[]{:S(2)}, u32[]{:S(2)}) collective-permute-start(bf16[64,2560]{1,0:T(8,128)(2,1)} %get-tuple-element.28), channel_id=1, source_target_pairs={{1,0},{2,1},{3,2},{5,4},{6,5},{7,6},{9,8},{10,9},{11,10},{13,12},{... | collective-permute-start | bytes 983048 | tf_op jit(solution)/shard_map/ppermute | solution.py:15
  334.5 11.0 %copy-start.5 = (f32[64,20,128]{2,1,0:T(8,128)}, f32[64,20,128]{2,1,0:T(8,128)S(1)}, u32[]{:S(2)}) copy-start(f32[64,20,128]{2,1,0:T(8,128)S(1)} %reshape.574) | copy-start | bytes 1966084
  342.0 3.5 copy-start.60
  352.4 4.4 copy-start.36
  356.8 2.9 copy-start.41
  356.8 2.9 copy-start.54
  364.2 15.3 %collective-permute-start.6 = (bf16[64,2560]{1,0:T(8,128)(2,1)}, bf16[64,2560]{1,0:T(8,128)(2,1)}, u32[]{:S(2)}, u32[]{:S(2)}) collective-permute-start(bf16[64,2560]{1,0:T(8,128)(2,1)} %get-tuple-element.26), channel_id=1, source_target_pairs={{1,0},{2,1},{3,2},{5,4},{6,5},{7,6},{9,8},{10,9},{11,10},{13,12},{... | collective-permute-start | bytes 983048 | tf_op jit(solution)/shard_map/ppermute | solution.py:15
  382.4 3.5 copy-start.61
  404.6 9.0 %collective-permute-start.7 = (bf16[64,2560]{1,0:T(8,128)(2,1)S(1)}, bf16[64,2560]{1,0:T(8,128)(2,1)S(1)}, u32[]{:S(2)}, u32[]{:S(2)}) collective-permute-start(bf16[64,2560]{1,0:T(8,128)(2,1)S(1)} %get-tuple-element.24), channel_id=1, source_target_pairs={{1,0},{2,1},{3,2},{5,4},{6,5},{7,6},{9,8},{10,9},{11,10},{13,12},{... | collective-permute-start | bytes 983048 | tf_op jit(solution)/shard_map/ppermute | solution.py:15
  444.4 4.4 copy-start.23
  444.4 4.4 copy-start.31
  454.0 4.6 copy-start.33
  454.0 4.6 copy-start.34
  (24 other events, 48.0 us)
Sparse Core Ops, SparseCore 0:
  11.3 85.8 all-gather.1
  467.6 149.5 reduce-scatter.4
where the time goes:
time: 636 us; the launch traced here: 626 us
  waiting for transfers between devices  254 us (40%)
  matrix products  128 us (20%)
  local copies, waits for them, and re-layouts  126 us (20%)
  other arithmetic  80.1 us (13%)
  starting transfers between devices  22.5 us (4%)
  between operations  15.2 us (2%)
    unnamed x3, waiting for transfers between devices  146 us
    all_gather x1, waiting for transfers between devices, shards(): gathered = lax.all_gather(packed, 'dp', axis=1, tiled=True)[0]  84.3 us
    dot_general x19, matrix products, panel_product(): jnp.einsum('brc,bp->prc', products, placing, precision=lax.Precision.HIGH)  71.4 us
    dot_general x19, matrix products, panel_product(): jnp.einsum(form, picked, blocks, preferred_element_type=jnp.float32)  51.1 us
    gather x19, local copies, waits for them, and re-layouts, panel_product(): picked = jnp.take(panels, pick_index, axis=0)  49 us
    unnamed x20, other arithmetic  41 us
    unnamed x131, local copies, waits for them, and re-layouts  28.9 us
    ppermute x8, waiting for transfers between devices, from_behind(): return lax.ppermute(value, axis, pairs)  23.9 us
  transfers between devices with their start and end apart: 10, of which 8 were waited for; matrix products, arithmetic and copies ran while one was open for 11% of the time, Pallas kernels for 0%

commit v1 on v0

--- a/solution.py
+++ b/solution.py
@@ -7,6 +7,18 @@
 FF = 10240
 MICRO = 2
 epsilon = 1e-05
+
+
+def view_sector(array_in):
+    return jnp.concatenate(
+        lax.all_to_all(
+            jnp.stack([array_in for _ in range(lax.axis_size("dp"))], axis=0),
+            "dp",
+            split_axis=0,
+            concat_axis=0,
+        ),
+        axis=1,
+    )
 
 
 def from_behind(value, axis, by):
@@ -143,7 +155,7 @@
         ],
         axis=2,
     )
-    gathered = lax.all_gather(packed, "dp", axis=1, tiled=True)[0]
+    gathered = view_sector(packed)[0]
     block_count = gathered.shape[0]
     up_blocks = gathered[:, :block_width].reshape(block_count, panel_width, panel_width)
     down_blocks = gathered[:, block_width : 2 * block_width].reshape(

time: 636 us -> 729 us (1.15)
  local copies, waits for them, and re-layouts: 126 us -> 168 us
  other arithmetic: 80.1 us -> 108 us
  starting transfers between devices: 22.5 us -> 35.4 us
  waiting for transfers between devices: 254 us -> 265 us
    all_to_all x0 -> x1, waiting for transfers between devices: none -> 94.7 us  [view_sector(): lax.all_to_all(jnp.stack([array_in for _ in range(lax.axis_size('dp'))],...]
    all_gather x1 -> x0, waiting for transfers between devices: 84.3 us -> none  [shards(): gathered = lax.all_gather(packed, 'dp', axis=1, tiled=True)[0]]
    unnamed x131 -> x141, local copies, waits for them, and re-layouts: 28.9 us -> 60.3 us
    another operation x0 -> x1, other arithmetic: none -> 27.2 us  [view_sector(): jnp.stack([array_in for _ in range(lax.axis_size('dp'))], axis=0)]
    all_to_all x0 -> x1, starting transfers between devices: none -> 12.3 us  [view_sector(): lax.all_to_all(jnp.stack([array_in for _ in range(lax.axis_size('dp'))],...]
    unnamed x3 -> x2, waiting for transfers between devices: 146 us -> 147 us
  transfers between devices with their start and end apart: 10 -> 10, of which waited for: 8 -> 8; matrix products, arithmetic and copies ran while one was open for 11% -> 9% of each run, Pallas kernels for 0% -> 0%
where the time goes in v1:
time: 729 us; the launch traced here: 721 us
  waiting for transfers between devices  265 us (36%)
  local copies, waits for them, and re-layouts  168 us (23%)
  matrix products  130 us (18%)
  other arithmetic  108 us (15%)
  starting transfers between devices  35.4 us (5%)
  between operations  15.3 us (2%)
    unnamed x2, waiting for transfers between devices  147 us
    all_to_all x1, waiting for transfers between devices, view_sector(): lax.all_to_all(jnp.stack([array_in for _ in range(lax.axis_size('dp'))],...  94.7 us
    dot_general x19, matrix products, panel_product(): jnp.einsum('brc,bp->prc', products, placing, precision=lax.Precision.HIGH)  72.7 us
    unnamed x141, local copies, waits for them, and re-layouts  60.3 us
    dot_general x19, matrix products, panel_product(): jnp.einsum(form, picked, blocks, preferred_element_type=jnp.float32)  51.1 us
    gather x19, local copies, waits for them, and re-layouts, panel_product(): picked = jnp.take(panels, pick_index, axis=0)  49.5 us
    unnamed x20, other arithmetic  41 us
    another operation x1, other arithmetic, view_sector(): jnp.stack([array_in for _ in range(lax.axis_size('dp'))], axis=0)  27.2 us
  transfers between devices with their start and end apart: 10, of which 8 were waited for; matrix products, arithmetic and copies ran while one was open for 9% of the time, Pallas kernels for 0%

profile of v1, /device:TPU:8, one launch (start us, length us, event | category | flops | bytes accessed | tf_op | source)
XLA Modules:
  0.0 721.0 jit_solution(3911748816636401525)
XLA Ops:
  9.8 5.6 stack.72
  15.9 27.2 %reduce.12 = bf16[64,32896]{1,0:T(8,128)(2,1)} reduce(bf16[64,1,1,32896]{3,2,1,0:T(2,128)(2,1)} %stack.72, bf16[]{:T(256)} %broadcast.595), dimensions={1,2}, to_apply=%stack.72.reduce_sub_computation | reduce | bytes 8421378 | tf_op jit(solution)/shard_map/stack | solution.py:15
  43.1 7.8 %reshape.843 = bf16[64,2,16448]{2,1,0:T(2,128)(2,1)} reshape(bf16[64,32896]{1,0:T(8,128)(2,1)} %reduce.12) | data formatting | bytes 8421376
  51.0 12.3 %all-to-all-start = ((bf16[64,2,16448]{2,1,0:T(2,128)(2,1)}), bf16[64,2,16448]{2,1,0:T(2,128)(2,1)}, u32[]{:S(2)}, u32[]{:S(2)}) async-start(bf16[64,2,16448]{2,1,0:T(2,128)(2,1)} %reshape.843), calls=%async_computation | async-start | bytes 8454144 | tf_op jit(solution)/shard_map/all_to_all | solution.py:14
  65.0 94.7 %all-to-all-done = bf16[64,2,16448]{2,1,0:T(2,128)(2,1)} async-done(((bf16[64,2,16448]{2,1,0:T(2,128)(2,1)}), bf16[64,2,16448]{2,1,0:T(2,128)(2,1)}, u32[]{:S(2)}, u32[]{:S(2)}) %all-to-all-start) | async-done | bytes 4210720 | tf_op jit(solution)/shard_map/all_to_all | solution.py:14
  159.7 24.5 %reshape.844 = bf16[64,1,1,32896]{3,2,1,0:T(2,128)(2,1)} reshape(bf16[64,2,16448]{2,1,0:T(2,128)(2,1)} %all-to-all-done) | data formatting | bytes 8421376
  184.2 3.8 copy.256
  196.6 3.5 bitcast_dynamic-update-slice_fusion.4
  211.7 3.7 collective-permute-start
  216.3 7.1 collective-permute-done
  228.2 3.5 bitcast_dynamic-update-slice_fusion.3
  242.1 3.7 collective-permute-start.1
  246.7 6.6 collective-permute-done.1
  261.3 3.5 bitcast_dynamic-update-slice_fusion.2
  275.2 3.9 collective-permute-start.2
  293.4 3.6 bitcast_dynamic-update-slice_fusion.1
  306.6 3.6 collective-permute-start.3
  320.5 3.6 bitcast_dynamic-update-slice_fusion
  324.1 3.8 fusion.201
  327.9 6.7 bitcast_dynamic-update-slice_fusion.9
  342.0 3.1 gather_fusion.11
  358.0 3.3 dynamic-slice_convert_fusion
  368.3 3.7 fusion.200
  372.0 3.7 fusion.199
  375.6 3.8 fusion.198
  381.3 3.7 fusion.197
  392.3 3.5 fusion.216
  395.8 6.9 bitcast_dynamic-update-slice_fusion.8
  417.1 3.4 constant_dynamic-slice_fusion.2
  429.2 3.5 fusion.212
  432.7 7.1 bitcast_dynamic-update-slice_fusion.7
  441.2 3.1 gather_fusion.15
  457.8 3.9 copy.114
  461.7 4.0 gather_fusion.20
  470.4 3.5 fusion.208
  473.9 6.9 bitcast_dynamic-update-slice_fusion.6
  482.2 3.1 gather_fusion.17
  498.6 3.4 collective-permute-done.7
  504.6 3.5 fusion.204
  508.1 6.9 bitcast_dynamic-update-slice_fusion.5
  516.4 3.1 gather_fusion.22
  529.4 4.2 gather_fusion.19
  536.2 4.4 copy.258
  543.1 3.2 fusion.133
  546.4 4.7 copy.257
  551.2 3.8 fusion
  555.0 4.9 copy.143
  564.5 147.3 %reduce-scatter.5.cloned.1.call-done = f32[1,1,264,128]{3,2,1,0:T(8,128)} async-done(((f32[1,64,264,128]{3,2,1,0:T(8,128)}), f32[1,1,264,128]{3,2,1,0:T(8,128)}) %reduce-scatter.5.cloned.1.call-update) | async-done | bytes 135184
  (288 shorter events, 213.4 us)
Async XLA Ops:
  51.0 12.5 %copy-start.2 = (bf16[128,2560]{1,0:T(8,128)(2,1)S(1)}, bf16[128,2560]{1,0:T(8,128)(2,1)}, u32[]{:S(2)}) copy-start(bf16[128,2560]{1,0:T(8,128)(2,1)} %param.14) | copy-start | bytes 1966084
  51.0 12.7 %copy-start.50 = (s32[1,4,64]{2,1,0:T(4,128)S(1)}, s32[1,4,64]{2,1,0:T(4,128)}, u32[]{:S(2)}) copy-start(s32[1,4,64]{2,1,0:T(4,128)} %param.18) | copy-start | bytes 3076
  51.0 108.7 %all-to-all-start = ((bf16[64,2,16448]{2,1,0:T(2,128)(2,1)}), bf16[64,2,16448]{2,1,0:T(2,128)(2,1)}, u32[]{:S(2)}, u32[]{:S(2)}) async-start(bf16[64,2,16448]{2,1,0:T(2,128)(2,1)} %reshape.843), calls=%async_computation | async-start | bytes 8454144 | tf_op jit(solution)/shard_map/all_to_all | solution.py:14
  63.3 648.6 %reduce-scatter.5.cloned.1.call-start = ((), (), s32[]{:S(2)}) async-start(), calls=%async_computation.2 | async-start | bytes 8785920
  64.2 238.0 %copy-start.45 = (pred[64]{0:T(512)(128)(4,1)}, pred[64]{0:T(512)(128)(4,1)S(1)}, u32[]{:S(2)}) copy-start(pred[64]{0:T(512)(128)(4,1)S(1)} %get-tuple-element.60) | copy-start | bytes 196
  64.2 254.3 %copy-start.39 = (pred[64]{0:T(512)(128)(4,1)}, pred[64]{0:T(512)(128)(4,1)S(1)}, u32[]{:S(2)}) copy-start(pred[64]{0:T(512)(128)(4,1)S(1)} %get-tuple-element.62) | copy-start | bytes 196
  64.2 235.0 %copy-start.49 = (s32[1024]{0:T(1024)}, s32[1024]{0:T(1024)S(1)}, u32[]{:S(2)}) copy-start(s32[1024]{0:T(1024)S(1)} %get-tuple-element.91) | copy-start | bytes 12292
  64.2 252.6 %copy-start.47 = (s32[1024]{0:T(1024)}, s32[1024]{0:T(1024)S(1)}, u32[]{:S(2)}) copy-start(s32[1024]{0:T(1024)S(1)} %get-tuple-element.92) | copy-start | bytes 12292
  65.0 262.9 %copy-start.62 = (s32[64]{0:T(128)}, s32[64]{0:T(128)S(1)}, u32[]{:S(2)}) copy-start(s32[64]{0:T(128)S(1)} %get-tuple-element.59) | copy-start | bytes 772
  211.7 11.7 %collective-permute-start = (bf16[64,2560]{1,0:T(8,128)(2,1)S(1)}, bf16[64,2560]{1,0:T(8,128)(2,1)S(1)}, u32[]{:S(2)}, u32[]{:S(2)}) collective-permute-start(bf16[64,2560]{1,0:T(8,128)(2,1)S(1)} %fusion.309), channel_id=1, source_target_pairs={{0,1},{1,2},{2,3},{4,5},{5,6},{6,7},{8,9},{9,10},{10,11},{12,13},{... | collective-permute-start | bytes 983048 | tf_op jit(solution)/shard_map/ppermute | solution.py:27
  216.3 100.4 %copy-start.24 = (f32[2560]{0:T(1024)}, f32[2560]{0:T(1024)S(1)}, u32[]{:S(2)}) copy-start(f32[2560]{0:T(1024)S(1)} %reshape.568) | copy-start | bytes 30724
  224.2 4.0 copy-start.16
  239.6 6.2 copy-start.1
  242.1 11.2 %collective-permute-start.1 = (bf16[64,2560]{1,0:T(8,128)(2,1)}, bf16[64,2560]{1,0:T(8,128)(2,1)}, u32[]{:S(2)}, u32[]{:S(2)}) collective-permute-start(bf16[64,2560]{1,0:T(8,128)(2,1)} %fusion.282), channel_id=1, source_target_pairs={{0,1},{1,2},{2,3},{4,5},{5,6},{6,7},{8,9},{9,10},{10,11},{12,13},{... | collective-permute-start | bytes 983048 | tf_op jit(solution)/shard_map/ppermute | solution.py:27
  275.2 10.3 %collective-permute-start.2 = (bf16[64,2560]{1,0:T(8,128)(2,1)}, bf16[64,2560]{1,0:T(8,128)(2,1)}, u32[]{:S(2)}, u32[]{:S(2)}) collective-permute-start(bf16[64,2560]{1,0:T(8,128)(2,1)} %fusion.286), channel_id=1, source_target_pairs={{0,1},{1,2},{2,3},{4,5},{5,6},{6,7},{8,9},{9,10},{10,11},{12,13},{... | collective-permute-start | bytes 983048 | tf_op jit(solution)/shard_map/ppermute | solution.py:27
  279.7 11.8 %copy-start.48 = (s32[1024]{0:T(1024)}, s32[1024]{0:T(1024)S(1)}, u32[]{:S(2)}) copy-start(s32[1024]{0:T(1024)S(1)} %get-tuple-element.90) | copy-start | bytes 12292
  304.9 5.4 copy-start
  304.9 5.4 copy-start.20
  306.6 9.0 %collective-permute-start.3 = (bf16[64,2560]{1,0:T(8,128)(2,1)S(1)}, bf16[64,2560]{1,0:T(8,128)(2,1)S(1)}, u32[]{:S(2)}, u32[]{:S(2)}) collective-permute-start(bf16[64,2560]{1,0:T(8,128)(2,1)S(1)} %fusion.290), channel_id=1, source_target_pairs={{0,1},{1,2},{2,3},{4,5},{5,6},{6,7},{8,9},{9,10},{10,11},{12,13},{... | collective-permute-start | bytes 983048 | tf_op jit(solution)/shard_map/ppermute | solution.py:27
  324.1 3.8 copy-start.23
  345.1 3.7 copy-start.41
  347.9 4.7 copy-start.25
  351.7 6.2 copy-start.26
  351.7 6.2 copy-start.52
  354.6 33.2 %collective-permute-start.4 = (bf16[64,2560]{1,0:T(8,128)(2,1)}, bf16[64,2560]{1,0:T(8,128)(2,1)}, u32[]{:S(2)}, u32[]{:S(2)}) collective-permute-start(bf16[64,2560]{1,0:T(8,128)(2,1)} %fusion.276), channel_id=1, source_target_pairs={{1,0},{2,1},{3,2},{5,4},{6,5},{7,6},{9,8},{10,9},{11,10},{13,12},{... | collective-permute-start | bytes 983048 | tf_op jit(solution)/shard_map/ppermute | solution.py:27
  358.0 5.4 copy-start.61
  365.1 15.2 %copy-start.9 = (f32[64,20,128]{2,1,0:T(8,128)}, f32[64,20,128]{2,1,0:T(8,128)S(1)}, u32[]{:S(2)}) copy-start(f32[64,20,128]{2,1,0:T(8,128)S(1)} %reshape.573) | copy-start | bytes 1966084
  365.8 14.6 %copy-start.56 = (f32[64]{0:T(128)}, f32[64]{0:T(128)S(1)}, u32[]{:S(2)}) copy-start(f32[64]{0:T(128)S(1)} %add_rsqrt_fusion.3) | copy-start | bytes 772
  375.6 3.8 copy-start.11
  375.6 3.8 copy-start.58
  386.2 9.6 %copy-start.7 = (f32[64,20,128]{2,1,0:T(8,128)}, f32[64,20,128]{2,1,0:T(8,128)S(1)}, u32[]{:S(2)}) copy-start(f32[64,20,128]{2,1,0:T(8,128)S(1)} %reshape.575) | copy-start | bytes 1966084
  392.3 3.5 copy-start.63
  402.7 4.5 copy-start.36
  415.2 9.5 %collective-permute-start.5 = (bf16[64,2560]{1,0:T(8,128)(2,1)}, bf16[64,2560]{1,0:T(8,128)(2,1)}, u32[]{:S(2)}, u32[]{:S(2)}) collective-permute-start(bf16[64,2560]{1,0:T(8,128)(2,1)} %get-tuple-element.28), channel_id=1, source_target_pairs={{1,0},{2,1},{3,2},{5,4},{6,5},{7,6},{9,8},{10,9},{11,10},{13,12},{... | collective-permute-start | bytes 983048 | tf_op jit(solution)/shard_map/ppermute | solution.py:27
  421.7 11.0 %copy-start.5 = (f32[64,20,128]{2,1,0:T(8,128)}, f32[64,20,128]{2,1,0:T(8,128)S(1)}, u32[]{:S(2)}) copy-start(f32[64,20,128]{2,1,0:T(8,128)S(1)} %reshape.577) | copy-start | bytes 1966084
  439.8 4.6 copy-start.37
  452.3 15.2 %collective-permute-start.6 = (bf16[64,2560]{1,0:T(8,128)(2,1)}, bf16[64,2560]{1,0:T(8,128)(2,1)}, u32[]{:S(2)}, u32[]{:S(2)}) collective-permute-start(bf16[64,2560]{1,0:T(8,128)(2,1)} %get-tuple-element.26), channel_id=1, source_target_pairs={{1,0},{2,1},{3,2},{5,4},{6,5},{7,6},{9,8},{10,9},{11,10},{13,12},{... | collective-permute-start | bytes 983048 | tf_op jit(solution)/shard_map/ppermute | solution.py:27
  493.1 9.0 %collective-permute-start.7 = (bf16[64,2560]{1,0:T(8,128)(2,1)S(1)}, bf16[64,2560]{1,0:T(8,128)(2,1)S(1)}, u32[]{:S(2)}, u32[]{:S(2)}) collective-permute-start(bf16[64,2560]{1,0:T(8,128)(2,1)S(1)} %get-tuple-element.24), channel_id=1, source_target_pairs={{1,0},{2,1},{3,2},{5,4},{6,5},{7,6},{9,8},{10,9},{11,10},{13,12},{... | collective-permute-start | bytes 983048 | tf_op jit(solution)/shard_map/ppermute | solution.py:27
  529.4 4.2 copy-start.3
  529.4 4.2 copy-start.38
  529.4 4.2 copy-start.40
  536.2 4.4 copy-start.22
  536.2 4.4 copy-start.30
  546.3 4.7 copy-start.31
  546.3 4.7 copy-start.32
  546.3 4.7 copy-start.33
  546.4 4.7 copy-start.34
  546.4 4.7 copy-start.35
  (28 other events, 61.4 us)
Sparse Core Ops, SparseCore 0:
  560.0 151.7 reduce-scatter.4
